TPU v7x, 32 devices: a whole 2x2x4 slice. The times are simulated.
32 devices in a mesh: grp: 4 (over z), emb: 8 (over y, x, core).
Axes of the slice: x: 2, y: 2, z: 4, core: 2. Of those that a mesh axis runs over, the one named last changes fastest.
Arguments:
- bottom_out: bfloat16 [4096, 128], P(('grp', 'emb')), may hold values from -6 to 6
- owner_ids: int32 [106496, 1], P(('grp', 'emb')), may hold values from 0 to 7; in each aligned block of 3328 rows (0 to 3327, 3328 to 6655, ...) at most 624 rows name the same one
- row_ids: int32 [4096, 26], P(('grp', 'emb')), may hold values from 0 to 95
- positions: int32 [4096], P(('grp', 'emb')), may hold values from 0 to 15
- labels: int32 [4096], P(('grp', 'emb')), may hold values 0 or 1
- tables: bfloat16 [26, 768, 128], P(None, 'emb'), may hold values from -6 to 6
- cross_down: bfloat16 [3456, 512], replicated, may hold values from -0.109375 to 0.109375
- cross_up: bfloat16 [512, 3456], replicated, may hold values from -0.25 to 0.25
- cross_bias: float32 [3456], replicated, may hold values from -3 to 3
- out_weight: bfloat16 [3456], replicated, may hold values from -0.109375 to 0.109375
- position_bias: float32 [16], replicated, may hold values from -2 to 2
Outputs:
- table_grad: float32 [26, 768, 128], P(None, 'emb')
- bottom_grad: bfloat16 [4096, 128], P(('grp', 'emb'))
- bias_grad: float32 [3456], replicated
Inputs may be any that keep to these rules, and one draw needn't show every extreme that they name: `owner_ids`: in every aligned block of 3328 lookups (the lookups of one device) no owner is named more than 624 times, and in some block one owner is named exactly 624 times.
All inputs are finite; a program needn't handle non-finite values. No bound on the sum of `labels` on one device may be relied on, other than what follows from the above.
Results may differ from a plain program's by a relative error of at most 0.0085.
Values may be sent and summed in bfloat16 or wider, within the bound.
No kernel may reach another device: no remote copies, remote signals or barrier semaphores. Data moves between devices by JAX's collectives and lax.ppermute only.
A program may use at most 64 MiB of HBM per device.

v0:
```python
import jax
import jax.numpy as jnp
from jax import lax
from jax.sharding import PartitionSpec as P


def local(
    bottom_out,
    owner_ids,
    row_ids,
    positions,
    labels,
    tables,
    cross_down,
    cross_up,
    cross_bias,
    out_weight,
    position_bias,
):
    sample_count, table_count = row_ids.shape
    rows_local = tables.shape[1]
    row_width = tables.shape[2]
    owner_count = lax.axis_size("emb")
    capacity = 3 * sample_count * table_count // (2 * owner_count)
    lookup_count = sample_count * table_count
    owners = owner_ids.reshape(sample_count, table_count)
    flat_owner = owners.reshape(-1)
    local_grid = jnp.arange(table_count, dtype=jnp.int32)[None, :] * rows_local + row_ids
    local_index = local_grid.reshape(-1)
    owner_marks = (flat_owner[:, None] == jnp.arange(owner_count, dtype=jnp.int32)[None, :]).astype(
        jnp.int32
    )
    ranking = jnp.cumsum(owner_marks, axis=0) - 1
    slot_index = jnp.sum(ranking * owner_marks, axis=1)
    buffer_place = flat_owner * capacity + slot_index
    flat_table = tables.reshape(table_count * rows_local, row_width)
    request = jnp.zeros((owner_count * capacity,), jnp.int32).at[buffer_place].set(local_index)
    request = request.reshape(owner_count, capacity)
    received = lax.all_to_all(request, "emb", split_axis=0, concat_axis=0, tiled=True)
    fetched = flat_table[received]
    arrived = lax.all_to_all(fetched, "emb", split_axis=0, concat_axis=0, tiled=True)
    pooled = arrived.reshape(owner_count * capacity, row_width)[buffer_place].reshape(
        sample_count, table_count * row_width
    )
    first = jnp.concatenate([bottom_out, pooled], axis=1)
    first_wide = first.astype(jnp.float32)
    weight_row = out_weight.astype(jnp.float32)
    reduced = jnp.dot(first, cross_down, preferred_element_type=jnp.float32).astype(jnp.bfloat16)
    gate_scale = jnp.dot(reduced, cross_up, preferred_element_type=jnp.float32) + cross_bias
    crossed = first_wide * gate_scale + first_wide
    position_marks = (
        positions[:, None] == jnp.arange(position_bias.shape[0], dtype=jnp.int32)[None, :]
    ).astype(jnp.float32)
    logit = jnp.sum(crossed * weight_row[None, :], axis=1) + jnp.sum(
        position_marks * position_bias[None, :], axis=1
    )
    err = jax.nn.sigmoid(logit) - labels.astype(jnp.float32)
    cotangent = err[:, None] * weight_row[None, :]
    scaled = cotangent * first_wide
    down_grad = lax.dot_general(
        scaled.astype(jnp.bfloat16),
        cross_up,
        (((1,), (1,)), ((), ())),
        preferred_element_type=jnp.float32,
    ).astype(jnp.bfloat16)
    back_term = lax.dot_general(
        down_grad, cross_down, (((1,), (1,)), ((), ())), preferred_element_type=jnp.float32
    )
    input_grad = (cotangent * (gate_scale + 1.0) + back_term).astype(jnp.bfloat16)
    bottom_grad = input_grad[:, :row_width]
    row_grads = input_grad[:, row_width:].reshape(lookup_count, row_width)
    outgoing = (
        jnp.zeros((owner_count * capacity, row_width), jnp.bfloat16).at[buffer_place].set(row_grads)
    )
    incoming = lax.all_to_all(
        outgoing.reshape(owner_count, capacity, row_width),
        "emb",
        split_axis=0,
        concat_axis=0,
        tiled=True,
    )
    local_grad = (
        jnp.zeros((table_count * rows_local, row_width), jnp.float32)
        .at[received.reshape(-1)]
        .add(incoming.reshape(owner_count * capacity, row_width).astype(jnp.float32))
    )
    summed_grad = lax.psum(local_grad.astype(jnp.bfloat16), "grp").astype(jnp.float32)
    table_grad = summed_grad.reshape(table_count, rows_local, row_width)
    bias_local = jnp.sum(scaled, axis=0)
    bias_grad = lax.psum(bias_local, ("grp", "emb"))
    return (table_grad, bottom_grad, bias_grad)


def solution(mesh):
    placed = (
        P(("grp", "emb"), None),
        P(("grp", "emb"), None),
        P(("grp", "emb"), None),
        P(("grp", "emb")),
        P(("grp", "emb")),
        P(None, "emb", None),
        P(),
        P(),
        P(),
        P(),
        P(),
    )
    return jax.shard_map(
        local,
        mesh=mesh,
        in_specs=placed,
        out_specs=(P(None, "emb", None), P(("grp", "emb"), None), P()),
        check_vma=False,
    )
```

profile of v0, /device:TPU:0, one launch (start us, length us, event | category | flops | bytes accessed | tf_op | source)
XLA Modules:
  0.0 242.6 jit_solution(920060485825970964)
XLA Ops:
  8.9 1.6 reshape.157
  11.9 5.2 %reduce-window.6 = s32[8,26,128]{2,1,0:T(8,128)} reduce-window(s32[8,26,128]{2,1,0:T(8,128)} %fusion.17, s32[]{:T(128)} %constant.10.clone.1), window={size=1x1x128 pad=0_0x0_0x127_0}, to_apply=%region_0.0 | reduce-window | flops 3381248 | bytes 212996 | tf_op jit(solution)/shard_map/reduce-window
  17.1 1.8 slice_reduce_fusion
  18.9 1.5 reduce-window.9
  22.2 13.5 %scatter_custom_fusion = s32[4992]{0:T(1024)} fusion(s32[3328]{0:T(1024)S(1)} %fusion.22, s32[3328]{0:T(1024)} %reshape.157, s32[]{:T(128)} %constant.10.clone.1), kind=kCustom, calls=%fused_computation.40 | custom fusion | bytes 20480 | tf_op jit(solution)/shard_map/scatter | solution.py:37
  37.1 9.9 %all_to_all.22 = s32[8,1,624]{2,1,0:T(1,128)S(1)} all-to-all(s32[8,1,624]{2,1,0:T(1,128)} %all_to_all.14), channel_id=1, replica_groups=mesh['grp'=4,'emb'=8] {'emb'}, dimensions={0} | all-to-all | bytes 39936 | tf_op jit(solution)/shard_map/all_to_all | solution.py:39
  51.1 12.3 %gather_fusion = bf16[4992,128]{1,0:T(8,128)(2,1)} fusion(bf16[2496,128]{1,0:T(8,128)(2,1)} %bitcast.32, s32[5120]{0:T(1024)} %pad_clamp_fusion), kind=kCustom, calls=%fused_computation | custom fusion | bytes 2575872 | tf_op jit(solution)/shard_map/gather | solution.py:40
  63.4 4.3 %all-to-all-start.1 = ((bf16[8,624,128]{2,1,0:T(8,128)(2,1)}), bf16[8,624,128]{2,1,0:T(8,128)(2,1)}, u32[]{:S(2)}, u32[]{:S(2)}) async-start(bf16[8,624,128]{2,1,0:T(8,128)(2,1)} %bitcast.34), calls=%async_computation.1 | async-start | bytes 2555904 | tf_op jit(solution)/shard_map/all_to_all | solution.py:41
  72.3 13.2 %all-to-all-done.1 = bf16[8,624,128]{2,1,0:T(8,128)(2,1)} async-done(((bf16[8,624,128]{2,1,0:T(8,128)(2,1)}), bf16[8,624,128]{2,1,0:T(8,128)(2,1)}, u32[]{:S(2)}, u32[]{:S(2)}) %all-to-all-start.1) | async-done | bytes 1277984 | tf_op jit(solution)/shard_map/all_to_all | solution.py:41
  85.5 9.2 %gather_fusion.1 = bf16[3328,128]{1,0:T(8,128)(2,1)} fusion(bf16[4992,128]{1,0:T(8,128)(2,1)} %bitcast.4, s32[4096]{0:T(1024)} %pad_clamp_fusion.1), kind=kCustom, calls=%fused_computation.1 | custom fusion | bytes 1717248 | tf_op jit(solution)/shard_map/gather | solution.py:42
  94.7 2.8 %reshape.131 = bf16[128,3328]{1,0:T(8,128)(2,1)} reshape(bf16[3328,128]{1,0:T(8,128)(2,1)} %gather_fusion.1) | data formatting | bytes 1703936 | tf_op jit(solution)/shard_map/reshape | solution.py:42
  97.5 2.1 constant_dynamic-update-slice_fusion
  99.6 5.6 %fusion.6 = (f32[128]{0:T(128)}, f32[128,3456]{1,0:T(8,128)}) fusion(bf16[128,3456]{1,0:T(8,128)(2,1)} %constant_dynamic-update-slice_fusion, f32[3456]{0:T(1024)S(1)} %convert_element_type.40, f32[3456]{0:T(1024)} %param.19, bf16[512,3456]{1,0:T(8,128)(2,1)} %param.18, bf16[3456,512]{1,0:T(8,128)(2,1)S(1)} %copy-done), kind=kOutput, calls=%fused_computation.16 | convolution fusion | flops 908689280 | bytes 9760256 | tf_op jit(solution)/shard_map/dot_general | solution.py:49
  106.4 6.1 %fusion = bf16[128,3456]{1,0:T(8,128)(2,1)} fusion(bf16[3456,512]{1,0:T(8,128)(2,1)S(1)} %copy-done, f32[128,3456]{1,0:T(8,128)} %get-tuple-element.4, bf16[512,3456]{1,0:T(8,128)(2,1)} %param.18, bf16[128,3456]{1,0:T(8,128)(2,1)} %constant_dynamic-update-slice_fusion, f32[128]{0:T(128)} %divide_subtract_fusion, f32[3456]{0:T(1024)S(1)} %convert_element_type.40), kind=kOutput, calls=%fused_computation.7 | convolution fusion | flops 910016512 | bytes 10631168 | tf_op jit(solution)/shard_map/dot_general | solution.py:66
  112.4 2.1 slice.21
  114.5 2.9 %reshape.165 = bf16[3328,128]{1,0:T(8,128)(2,1)} reshape(bf16[128,3328]{1,0:T(8,128)(2,1)} %slice.21) | data formatting | bytes 1703936 | tf_op jit(solution)/shard_map/reshape | solution.py:71
  117.4 14.9 %scatter_custom_fusion.1 = bf16[4992,128]{1,0:T(8,128)(2,1)} fusion(s32[3328]{0:T(1024)} %copy-done.2, bf16[3328,128]{1,0:T(8,128)(2,1)} %reshape.165, bf16[]{:T(256)} %constant.5.clone.1), kind=kCustom, calls=%fused_computation.21 | custom fusion | bytes 1278464 | tf_op jit(solution)/shard_map/scatter | solution.py:73
  132.3 4.3 %all-to-all-start.2 = ((bf16[8,624,128]{2,1,0:T(8,128)(2,1)}), bf16[8,624,128]{2,1,0:T(8,128)(2,1)}, u32[]{:S(2)}, u32[]{:S(2)}) async-start(bf16[8,624,128]{2,1,0:T(8,128)(2,1)} %bitcast.33), calls=%async_computation.2 | async-start | bytes 2555904 | tf_op jit(solution)/shard_map/all_to_all | solution.py:75
  141.0 13.4 %all-to-all-done.2 = bf16[8,624,128]{2,1,0:T(8,128)(2,1)} async-done(((bf16[8,624,128]{2,1,0:T(8,128)(2,1)}), bf16[8,624,128]{2,1,0:T(8,128)(2,1)}, u32[]{:S(2)}, u32[]{:S(2)}) %all-to-all-start.2) | async-done | bytes 1277984 | tf_op jit(solution)/shard_map/all_to_all | solution.py:75
  154.4 33.9 %scatter_custom_fusion.2 = f32[2496,128]{1,0:T(8,128)} fusion(s32[4992]{0:T(1024)} %fusion.21, bf16[4992,128]{1,0:T(8,128)(2,1)} %bitcast.8, f32[]{:T(128)} %constant.9.clone.1), kind=kCustom, calls=%fused_computation.9 | custom fusion | flops 1277952 | bytes 2556416 | tf_op jit(solution)/shard_map/scatter-add | solution.py:85
  188.4 2.2 convert_element_type.47
  192.0 2.1 fusion.3
  194.1 39.5 %psum.15 = f32[3456]{0:T(1024)} all-reduce(f32[3456]{0:T(1024)} %fusion.3), channel_id=1, replica_groups=mesh['grp'=4,'emb'=8] {'grp','emb'}, use_global_device_ids=true, to_apply=%region_10.11 | all-reduce | flops 3456 | bytes 27648 | tf_op jit(solution)/shard_map/psum | solution.py:90
  233.5 2.3 reshape.135
  (30 shorter events, 22.1 us)
Async XLA Ops:
  7.2 92.5 %copy-start = (bf16[3456,512]{1,0:T(8,128)(2,1)S(1)}, bf16[3456,512]{1,0:T(8,128)(2,1)}, u32[]{:S(2)}) copy-start(bf16[3456,512]{1,0:T(8,128)(2,1)} %param.17) | copy-start | bytes 10616836
  22.2 41.2 %copy-start.2 = (s32[3328]{0:T(1024)}, s32[3328]{0:T(1024)S(1)}, u32[]{:S(2)}) copy-start(s32[3328]{0:T(1024)S(1)} %fusion.22) | copy-start | bytes 39940
  47.1 0.6 copy-start.1
  63.4 22.1 %all-to-all-start.1 = ((bf16[8,624,128]{2,1,0:T(8,128)(2,1)}), bf16[8,624,128]{2,1,0:T(8,128)(2,1)}, u32[]{:S(2)}, u32[]{:S(2)}) async-start(bf16[8,624,128]{2,1,0:T(8,128)(2,1)} %bitcast.34), calls=%async_computation.1 | async-start | bytes 2555904 | tf_op jit(solution)/shard_map/all_to_all | solution.py:41
  132.3 22.1 %all-to-all-start.2 = ((bf16[8,624,128]{2,1,0:T(8,128)(2,1)}), bf16[8,624,128]{2,1,0:T(8,128)(2,1)}, u32[]{:S(2)}, u32[]{:S(2)}) async-start(bf16[8,624,128]{2,1,0:T(8,128)(2,1)} %bitcast.33), calls=%async_computation.2 | async-start | bytes 2555904 | tf_op jit(solution)/shard_map/all_to_all | solution.py:75
  136.5 97.0 %all-reduce.2.cloned.1.call-start = ((), (), s32[]{:S(2)}) async-start(), calls=%async_computation.3 | async-start | bytes 1277952 | tf_op jit(solution)/shard_map/psum | solution.py:87
Sparse Core Ops, SparseCore 0:
  190.7 39.9 all-reduce.1
where the time goes:
time: 245 us; the launch traced here: 243 us
  local copies, waits for them, and re-layouts  71.5 us (29%)
  other arithmetic  60.6 us (25%)
  blocking collectives  49.4 us (20%)
  waiting for transfers between devices  26.7 us (11%)
  between operations  14.1 us (6%)
  matrix products  11.6 us (5%)
  starting transfers between devices  8.73 us (4%)
    psum x1, blocking collectives, local(): bias_grad = lax.psum(bias_local, ('grp', 'emb'))  39.5 us
    scatter-add x1, other arithmetic, local(): local_grad = jnp.zeros((table_count * rows_local, row_width), jnp.float32...  33.9 us
    scatter x1, local copies, waits for them, and re-layouts, local(): jnp.zeros((owner_count * capacity, row_width), jnp.bfloat16)  14.9 us
    scatter x1, local copies, waits for them, and re-layouts, local(): jnp.zeros((owner_count * capacity,), jnp.int32).at[buffer_place]  13.5 us
    all_to_all x1, waiting for transfers between devices, local(): lax.all_to_all(outgoing.reshape(owner_count, capacity, row_width), 'emb',...  13.4 us
    all_to_all x1, waiting for transfers between devices, local(): lax.all_to_all(fetched, 'emb', split_axis=0, concat_axis=0, tiled=True)  13.2 us
    gather x1, local copies, waits for them, and re-layouts, local(): fetched = flat_table[received]  12.3 us
    all_to_all x1, blocking collectives, local(): lax.all_to_all(request, 'emb', split_axis=0, concat_axis=0, tiled=True)  9.94 us
  transfers between devices with their start and end apart: 3, of which 2 were waited for; matrix products, arithmetic and copies ran while one was open for 5% of the time, Pallas kernels for 0%

commit v1 on v0

--- a/solution.py
+++ b/solution.py
@@ -87,7 +87,9 @@
     summed_grad = lax.psum(local_grad.astype(jnp.bfloat16), "grp").astype(jnp.float32)
     table_grad = summed_grad.reshape(table_count, rows_local, row_width)
     bias_local = jnp.sum(scaled, axis=0)
-    bias_grad = lax.psum(bias_local, ("grp", "emb"))
+    bias_grad = bias_local
+    for mesh_axis in ("emb", "grp"):
+        bias_grad = lax.psum(bias_grad, mesh_axis)
     return (table_grad, bottom_grad, bias_grad)
 
 

time: 245 us -> 248 us (1.012)
  blocking collectives: 49.4 us -> 52.5 us
    psum x1 -> x2, blocking collectives: 39.5 us -> 42.5 us  [local(): bias_grad = lax.psum(bias_grad, mesh_axis)]
where the time goes in v1:
time: 248 us; the launch traced here: 246 us
  local copies, waits for them, and re-layouts  71.5 us (29%)
  other arithmetic  60.6 us (24%)
  blocking collectives  52.5 us (21%)
  waiting for transfers between devices  26.7 us (11%)
  between operations  14.1 us (6%)
  matrix products  11.6 us (5%)
  starting transfers between devices  8.73 us (4%)
    psum x2, blocking collectives, local(): bias_grad = lax.psum(bias_grad, mesh_axis)  42.5 us
    scatter-add x1, other arithmetic, local(): local_grad = jnp.zeros((table_count * rows_local, row_width), jnp.float32...  33.9 us
    scatter x1, local copies, waits for them, and re-layouts, local(): jnp.zeros((owner_count * capacity, row_width), jnp.bfloat16)  14.9 us
    scatter x1, local copies, waits for them, and re-layouts, local(): jnp.zeros((owner_count * capacity,), jnp.int32).at[buffer_place]  13.5 us
    all_to_all x1, waiting for transfers between devices, local(): lax.all_to_all(outgoing.reshape(owner_count, capacity, row_width), 'emb',...  13.4 us
    all_to_all x1, waiting for transfers between devices, local(): lax.all_to_all(fetched, 'emb', split_axis=0, concat_axis=0, tiled=True)  13.2 us
    gather x1, local copies, waits for them, and re-layouts, local(): fetched = flat_table[received]  12.3 us
    all_to_all x1, blocking collectives, local(): lax.all_to_all(request, 'emb', split_axis=0, concat_axis=0, tiled=True)  9.94 us
  transfers between devices with their start and end apart: 3, of which 2 were waited for; matrix products, arithmetic and copies ran while one was open for 5% of the time, Pallas kernels for 0%

profile of v1, /device:TPU:0, one launch (start us, length us, event | category | flops | bytes accessed | tf_op | source)
XLA Modules:
  0.0 245.7 jit_solution(15678349157538925956)
XLA Ops:
  8.9 1.6 reshape.157
  11.9 5.2 %reduce-window.6 = s32[8,26,128]{2,1,0:T(8,128)} reduce-window(s32[8,26,128]{2,1,0:T(8,128)} %fusion.17, s32[]{:T(128)} %constant.10.clone.1), window={size=1x1x128 pad=0_0x0_0x127_0}, to_apply=%region_0.0 | reduce-window | flops 3381248 | bytes 212996 | tf_op jit(solution)/shard_map/reduce-window
  17.1 1.8 slice_reduce_fusion
  22.2 13.5 %scatter_custom_fusion = s32[4992]{0:T(1024)} fusion(s32[3328]{0:T(1024)S(1)} %fusion.22, s32[3328]{0:T(1024)} %reshape.157, s32[]{:T(128)} %constant.10.clone.1), kind=kCustom, calls=%fused_computation.40 | custom fusion | bytes 20480 | tf_op jit(solution)/shard_map/scatter | solution.py:37
  37.1 9.9 %all_to_all.22 = s32[8,1,624]{2,1,0:T(1,128)S(1)} all-to-all(s32[8,1,624]{2,1,0:T(1,128)} %all_to_all.14), channel_id=1, replica_groups=mesh['grp'=4,'emb'=8] {'emb'}, dimensions={0} | all-to-all | bytes 39936 | tf_op jit(solution)/shard_map/all_to_all | solution.py:39
  51.1 12.3 %gather_fusion = bf16[4992,128]{1,0:T(8,128)(2,1)} fusion(bf16[2496,128]{1,0:T(8,128)(2,1)} %bitcast.32, s32[5120]{0:T(1024)} %pad_clamp_fusion), kind=kCustom, calls=%fused_computation | custom fusion | bytes 2575872 | tf_op jit(solution)/shard_map/gather | solution.py:40
  63.4 4.3 %all-to-all-start.1 = ((bf16[8,624,128]{2,1,0:T(8,128)(2,1)}), bf16[8,624,128]{2,1,0:T(8,128)(2,1)}, u32[]{:S(2)}, u32[]{:S(2)}) async-start(bf16[8,624,128]{2,1,0:T(8,128)(2,1)} %bitcast.34), calls=%async_computation.1 | async-start | bytes 2555904 | tf_op jit(solution)/shard_map/all_to_all | solution.py:41
  72.3 13.2 %all-to-all-done.1 = bf16[8,624,128]{2,1,0:T(8,128)(2,1)} async-done(((bf16[8,624,128]{2,1,0:T(8,128)(2,1)}), bf16[8,624,128]{2,1,0:T(8,128)(2,1)}, u32[]{:S(2)}, u32[]{:S(2)}) %all-to-all-start.1) | async-done | bytes 1277984 | tf_op jit(solution)/shard_map/all_to_all | solution.py:41
  85.5 9.2 %gather_fusion.1 = bf16[3328,128]{1,0:T(8,128)(2,1)} fusion(bf16[4992,128]{1,0:T(8,128)(2,1)} %bitcast.4, s32[4096]{0:T(1024)} %pad_clamp_fusion.1), kind=kCustom, calls=%fused_computation.1 | custom fusion | bytes 1717248 | tf_op jit(solution)/shard_map/gather | solution.py:42
  94.7 2.8 %reshape.131 = bf16[128,3328]{1,0:T(8,128)(2,1)} reshape(bf16[3328,128]{1,0:T(8,128)(2,1)} %gather_fusion.1) | data formatting | bytes 1703936 | tf_op jit(solution)/shard_map/reshape | solution.py:42
  97.5 2.1 constant_dynamic-update-slice_fusion
  99.6 5.6 %fusion.6 = (f32[128]{0:T(128)}, f32[128,3456]{1,0:T(8,128)}) fusion(bf16[128,3456]{1,0:T(8,128)(2,1)} %constant_dynamic-update-slice_fusion, f32[3456]{0:T(1024)S(1)} %convert_element_type.40, f32[3456]{0:T(1024)} %param.19, bf16[512,3456]{1,0:T(8,128)(2,1)} %param.18, bf16[3456,512]{1,0:T(8,128)(2,1)S(1)} %copy-done), kind=kOutput, calls=%fused_computation.16 | convolution fusion | flops 908689280 | bytes 9760256 | tf_op jit(solution)/shard_map/dot_general | solution.py:49
  106.4 6.1 %fusion = bf16[128,3456]{1,0:T(8,128)(2,1)} fusion(bf16[3456,512]{1,0:T(8,128)(2,1)S(1)} %copy-done, f32[128,3456]{1,0:T(8,128)} %get-tuple-element.4, bf16[512,3456]{1,0:T(8,128)(2,1)} %param.18, bf16[128,3456]{1,0:T(8,128)(2,1)} %constant_dynamic-update-slice_fusion, f32[128]{0:T(128)} %divide_subtract_fusion, f32[3456]{0:T(1024)S(1)} %convert_element_type.40), kind=kOutput, calls=%fused_computation.7 | convolution fusion | flops 910016512 | bytes 10631168 | tf_op jit(solution)/shard_map/dot_general | solution.py:66
  112.4 2.1 slice.21
  114.5 2.9 %reshape.165 = bf16[3328,128]{1,0:T(8,128)(2,1)} reshape(bf16[128,3328]{1,0:T(8,128)(2,1)} %slice.21) | data formatting | bytes 1703936 | tf_op jit(solution)/shard_map/reshape | solution.py:71
  117.4 14.9 %scatter_custom_fusion.1 = bf16[4992,128]{1,0:T(8,128)(2,1)} fusion(s32[3328]{0:T(1024)} %copy-done.2, bf16[3328,128]{1,0:T(8,128)(2,1)} %reshape.165, bf16[]{:T(256)} %constant.5.clone.1), kind=kCustom, calls=%fused_computation.21 | custom fusion | bytes 1278464 | tf_op jit(solution)/shard_map/scatter | solution.py:73
  132.3 4.3 %all-to-all-start.2 = ((bf16[8,624,128]{2,1,0:T(8,128)(2,1)}), bf16[8,624,128]{2,1,0:T(8,128)(2,1)}, u32[]{:S(2)}, u32[]{:S(2)}) async-start(bf16[8,624,128]{2,1,0:T(8,128)(2,1)} %bitcast.33), calls=%async_computation.2 | async-start | bytes 2555904 | tf_op jit(solution)/shard_map/all_to_all | solution.py:75
  141.0 13.4 %all-to-all-done.2 = bf16[8,624,128]{2,1,0:T(8,128)(2,1)} async-done(((bf16[8,624,128]{2,1,0:T(8,128)(2,1)}), bf16[8,624,128]{2,1,0:T(8,128)(2,1)}, u32[]{:S(2)}, u32[]{:S(2)}) %all-to-all-start.2) | async-done | bytes 1277984 | tf_op jit(solution)/shard_map/all_to_all | solution.py:75
  154.4 33.9 %scatter_custom_fusion.2 = f32[2496,128]{1,0:T(8,128)} fusion(s32[4992]{0:T(1024)} %fusion.21, bf16[4992,128]{1,0:T(8,128)(2,1)} %bitcast.8, f32[]{:T(128)} %constant.9.clone.1), kind=kCustom, calls=%fused_computation.9 | custom fusion | flops 1277952 | bytes 2556416 | tf_op jit(solution)/shard_map/scatter-add | solution.py:85
  188.4 2.2 convert_element_type.47
  192.0 2.1 fusion.3
  194.1 23.6 %psum.22 = f32[3456]{0:T(1024)S(1)} all-reduce(f32[3456]{0:T(1024)} %fusion.3), channel_id=1, replica_groups=mesh['grp'=4,'emb'=8] {'emb'}, use_global_device_ids=true, to_apply=%region_10.11 | all-reduce | flops 3456 | bytes 27648 | tf_op jit(solution)/shard_map/psum | solution.py:92
  217.7 18.9 %psum.23 = f32[3456]{0:T(1024)} all-reduce(f32[3456]{0:T(1024)S(1)} %psum.22), channel_id=1, replica_groups=mesh['grp'=4,'emb'=8] {'grp'}, use_global_device_ids=true, to_apply=%region_11.12 | all-reduce | flops 3456 | bytes 27648 | tf_op jit(solution)/shard_map/psum | solution.py:92
  236.6 2.3 reshape.135
  (31 shorter events, 23.5 us)
Async XLA Ops:
  7.2 92.5 %copy-start = (bf16[3456,512]{1,0:T(8,128)(2,1)S(1)}, bf16[3456,512]{1,0:T(8,128)(2,1)}, u32[]{:S(2)}) copy-start(bf16[3456,512]{1,0:T(8,128)(2,1)} %param.17) | copy-start | bytes 10616836
  22.2 41.2 %copy-start.2 = (s32[3328]{0:T(1024)}, s32[3328]{0:T(1024)S(1)}, u32[]{:S(2)}) copy-start(s32[3328]{0:T(1024)S(1)} %fusion.22) | copy-start | bytes 39940
  47.1 0.6 copy-start.1
  63.4 22.1 %all-to-all-start.1 = ((bf16[8,624,128]{2,1,0:T(8,128)(2,1)}), bf16[8,624,128]{2,1,0:T(8,128)(2,1)}, u32[]{:S(2)}, u32[]{:S(2)}) async-start(bf16[8,624,128]{2,1,0:T(8,128)(2,1)} %bitcast.34), calls=%async_computation.1 | async-start | bytes 2555904 | tf_op jit(solution)/shard_map/all_to_all | solution.py:41
  132.3 22.1 %all-to-all-start.2 = ((bf16[8,624,128]{2,1,0:T(8,128)(2,1)}), bf16[8,624,128]{2,1,0:T(8,128)(2,1)}, u32[]{:S(2)}, u32[]{:S(2)}) async-start(bf16[8,624,128]{2,1,0:T(8,128)(2,1)} %bitcast.33), calls=%async_computation.2 | async-start | bytes 2555904 | tf_op jit(solution)/shard_map/all_to_all | solution.py:75
  136.5 100.1 %all-reduce.2.cloned.1.call-start = ((), (), s32[]{:S(2)}) async-start(), calls=%async_computation.3 | async-start | bytes 1277952 | tf_op jit(solution)/shard_map/psum | solution.py:87
Sparse Core Ops, SparseCore 0:
  190.7 40.0 all-reduce.1
